TPU v7x, 256 devices: a whole 4x4x8 slice. The times are simulated.
256 devices in a mesh: rep: 8 (over y_hi, x), ep: 32 (over z, y_lo, core).
Axes of the slice: x: 4, y: 4 (y_hi: 2, y_lo: 2; y = y_hi * 2 + y_lo), z: 8, core: 2. Of those that a mesh axis runs over, the one named last changes fastest.
Arguments:
- queries: bfloat16 [8, 128, 36864], P('rep', None, 'ep'), may hold values from -64 to 64
- suffix_latent: bfloat16 [8, 73728], P('rep', 'ep'), may hold values from -4 to 4
- cache_pool: bfloat16 [8, 256, 36864], P('rep', 'ep'), may hold values from -4 to 4
- holders: int32 [8, 64], replicated, may hold values from 0 to 7, as said below
- block_slots: int32 [8, 64], replicated, may hold values from 0 to 7, as said below
- prefix_len: int32 [8], P('rep'), may hold values from 1024 to 4096, as said below
- hidden: bfloat16 [8, 128, 7168], P('rep', 'ep'), may hold values from -16 to 16
- w_value: bfloat16 [64, 512, 128], P('ep'), may hold values from -0.25 to 0.25
- w_out: bfloat16 [8192, 7168], P('ep'), may hold values from -0.0625 to 0.0625
- norm_gain: bfloat16 [7168], replicated, may hold values from 0.099609375 to 1.8984375
- experts: int32 [8, 128, 8], P('rep', 'ep'), may hold values from 0 to 31, all different within a row; in each aligned block of 4 rows (0 to 3, 4 to 7, ..., all dimensions but the last counted through in order) at most 2 rows name the same one
- gate_weights: bfloat16 [8, 128, 8], P('rep', 'ep'), may hold values from 0.029907227 to 0.29882812
- w_gate: bfloat16 [32, 7168, 1024], P('ep', None, 'rep'), may hold values from -0.0625 to 0.0625
- w_up: bfloat16 [32, 7168, 1024], P('ep', None, 'rep'), may hold values from -0.0625 to 0.0625
- w_down: bfloat16 [32, 1024, 7168], P('ep', 'rep'), may hold values from -0.1875 to 0.1875
Outputs:
- layer_out: float32 [8, 128, 7168], P('rep', 'ep')
Inputs may be any that keep to these rules, and one draw needn't show every extreme that they name: `holders`: for each group and each index s of ep, the blocks s * 2 to (s + 1) * 2 - 1 of its prefix come from holder groups none of which gives more than 1 of them. `block_slots`: block b of a prefix lies on index b // 2 of ep of its holder group. `prefix_len`: some group's prefix has 4096 tokens. Each row names 8 different experts; among the rows of one device no expert is named more than 2 times.
All inputs are finite; a program needn't handle non-finite values.
Results may differ from a plain program's by a relative error of at most 0.004.
Values may be sent and summed in bfloat16 or wider, within the bound.
No kernel may reach another device: no remote copies, remote signals or barrier semaphores. Data moves between devices by JAX's collectives and lax.ppermute only.
A program may use at most 128 MiB of HBM per device.

v0:
```python
import jax
import jax.numpy as jnp
from jax import lax
from jax.sharding import Mesh, PartitionSpec as P

KVR = 512
ROPE = 64
SUF = 128
EP = ("epo", "core")
score_scale = 0.07216878364870323
norm_eps = 1e-06


def expert_units(token_rows, gate_rows, up_rows):
    gate_part = jnp.dot(token_rows, gate_rows, preferred_element_type=jnp.float32)
    up_part = jnp.dot(token_rows, up_rows, preferred_element_type=jnp.float32)
    return (jax.nn.silu(gate_part) * up_part).astype(jnp.bfloat16)


def local(
    queries,
    suffix_latent,
    cache_pool,
    holders,
    block_slots,
    prefix_len,
    hidden,
    w_value,
    w_out,
    norm_gain,
    experts,
    gate_weights,
    w_gate,
    w_up,
    w_down,
):
    rep_count = lax.axis_size("rep")
    ep_count = lax.axis_size(EP)
    rep_index = lax.axis_index("rep")
    ep_index = lax.axis_index("epo") * lax.axis_size("core") + lax.axis_index("core")
    pool_count = cache_pool.shape[1]
    block_width = cache_pool.shape[2]
    per_device = holders.shape[1] // ep_count
    per_holder = (per_device + rep_count - 1) // rep_count
    latent_width = KVR + ROPE
    mine_holders = lax.dynamic_slice_in_dim(holders, ep_index * per_device, per_device, 1)
    mine_slots = lax.dynamic_slice_in_dim(block_slots, ep_index * per_device, per_device, 1)
    position = jnp.arange(per_device, dtype=jnp.int32)
    same_holder = mine_holders[:, :, None] == mine_holders[:, None, :]
    earlier = position[None, :] < position[:, None]
    occurrence = jnp.sum((same_holder & earlier[None, :, :]).astype(jnp.int32), axis=2)
    wanted = mine_holders == rep_index
    chosen_slot = occurrence[:, :, None] == jnp.arange(per_holder, dtype=jnp.int32)[None, None, :]
    chosen_row = mine_slots[:, :, None] == jnp.arange(pool_count, dtype=jnp.int32)[None, None, :]
    selector = jnp.einsum(
        "son,soh->snh",
        (wanted[:, :, None] & chosen_slot).astype(jnp.float32),
        chosen_row.astype(jnp.float32),
        precision=lax.Precision.HIGHEST,
    )
    outgoing = jnp.dot(
        selector.reshape(rep_count * per_holder, pool_count).astype(jnp.bfloat16),
        cache_pool[0],
        preferred_element_type=jnp.float32,
    )
    outgoing = outgoing.astype(jnp.bfloat16).reshape(rep_count, per_holder, block_width)
    incoming = lax.all_to_all(outgoing, "rep", split_axis=0, concat_axis=0, tiled=True)
    own_holders = lax.dynamic_index_in_dim(mine_holders, rep_index, 0, keepdims=False)
    own_order = lax.dynamic_index_in_dim(occurrence, rep_index, 0, keepdims=False)
    source = own_holders * per_holder + own_order
    picker = (
        source[:, None] == jnp.arange(rep_count * per_holder, dtype=jnp.int32)[None, :]
    ).astype(jnp.bfloat16)
    own_blocks = jnp.dot(
        picker,
        incoming.reshape(rep_count * per_holder, block_width),
        preferred_element_type=jnp.float32,
    ).astype(jnp.bfloat16)
    core_count = lax.axis_size("core")
    outer_count = ep_count // core_count
    pre_rows = per_device * (block_width // latent_width)
    suf_rows = SUF // ep_count
    pad_rows = -(pre_rows + suf_rows) % 16
    packed = jnp.concatenate(
        [
            own_blocks.reshape(pre_rows, latent_width),
            suffix_latent.reshape(suf_rows, latent_width),
            jnp.zeros((pad_rows, latent_width), own_blocks.dtype),
        ],
        axis=0,
    )
    row_count = packed.shape[0]
    chip_keys = lax.all_gather(packed[None], EP, axis=0, tiled=True)
    hidden_width, width = (w_down.shape[1], w_down.shape[2])
    chunk = width // rep_count
    down_cols = w_down[0].reshape(hidden_width, rep_count, chunk)
    down_cols = jnp.transpose(down_cols, (1, 0, 2))
    down_cols = lax.all_to_all(down_cols, "rep", 0, 0, tiled=True)
    gate_rows = lax.all_to_all(
        w_gate[0].reshape(rep_count, chunk, hidden_width), "rep", 0, 0, tiled=True
    )
    up_rows = lax.all_to_all(
        w_up[0].reshape(rep_count, chunk, hidden_width), "rep", 0, 0, tiled=True
    )
    chip_keys, down_cols, gate_rows, up_rows = lax.optimization_barrier(
        (chip_keys, down_cols, gate_rows, up_rows)
    )
    keys = chip_keys.reshape(-1, latent_width)
    device_of = lax.broadcasted_iota(jnp.int32, chip_keys.shape[:2], 0).reshape(-1)
    row_of = lax.broadcasted_iota(jnp.int32, chip_keys.shape[:2], 1).reshape(-1)
    is_prefix = (row_of < pre_rows) & (device_of * pre_rows + row_of < prefix_len[0])
    suffix_pos = device_of * suf_rows + row_of - pre_rows
    is_suffix = (row_of >= pre_rows) & (row_of < pre_rows + suf_rows)
    token_pos = jnp.arange(SUF, dtype=jnp.int32)
    visible = is_prefix[None, :] | is_suffix[None, :] & (suffix_pos[None, :] <= token_pos[:, None])
    query_rows = queries[0].reshape(SUF, -1, latent_width)
    scores = (
        jnp.einsum("thc,kc->htk", query_rows, keys, preferred_element_type=jnp.float32)
        * score_scale
    )
    scores = jnp.where(visible[None, :, :], scores, -1e30)
    highest = jnp.max(scores, axis=2)
    exps = jnp.exp(scores - highest[:, :, None])
    denominator = jnp.sum(exps, axis=2)
    latent = jnp.einsum(
        "htk,kc->thc", exps.astype(jnp.bfloat16), keys[:, :KVR], preferred_element_type=jnp.float32
    )
    latent = (latent / jnp.transpose(denominator)[:, :, None]).astype(jnp.bfloat16)
    head_values = jnp.einsum(
        "thc,hcv->thv", latent, w_value, preferred_element_type=jnp.float32
    ).astype(jnp.bfloat16)
    head_values = head_values.reshape(outer_count, core_count, suf_rows, -1)
    head_values = jnp.transpose(head_values, (1, 0, 2, 3)).reshape(SUF, -1)
    partial = jnp.dot(head_values, w_out, preferred_element_type=jnp.float32)
    partial = partial.reshape(core_count, SUF // core_count, -1)
    partial = lax.all_to_all(partial.astype(jnp.bfloat16), "core", 0, 0, tiled=True)
    partial = jnp.sum(partial.astype(jnp.float32), axis=0)
    partial = partial.reshape(outer_count, 16, -1).astype(jnp.bfloat16)
    attention = jnp.sum(
        lax.all_to_all(partial, "epo", 0, 0, tiled=True).astype(jnp.float32), axis=0
    )
    attention = attention.reshape(suf_rows, -1)
    residual = hidden[0].astype(jnp.float32) + attention
    scale_rows = lax.rsqrt(jnp.mean(residual * residual, axis=1, keepdims=True) + norm_eps)
    normed = (residual * scale_rows * norm_gain.astype(jnp.float32)).astype(jnp.bfloat16)
    tok_count = hidden.shape[1]
    chosen = experts[0]
    top_count = chosen.shape[1]
    expert_count = ep_count * w_gate.shape[0]
    capacity = min(tok_count, 2 * max(1, tok_count * top_count // expert_count))
    slot_count = expert_count * capacity
    flat_choice = chosen.reshape(-1)
    hits = (flat_choice[:, None] == jnp.arange(expert_count, dtype=jnp.int32)[None, :]).astype(
        jnp.int32
    )
    rank = jnp.sum((jnp.cumsum(hits, axis=0) - hits) * hits, axis=1)
    slot_id = flat_choice * capacity + rank
    slot_hot = (slot_id[:, None] == jnp.arange(slot_count, dtype=jnp.int32)[None, :]).astype(
        jnp.float32
    )
    owner = jnp.arange(flat_choice.shape[0], dtype=jnp.int32) // top_count
    token_hot = (owner[:, None] == jnp.arange(tok_count, dtype=jnp.int32)[None, :]).astype(
        jnp.float32
    )
    placing = jnp.dot(jnp.transpose(slot_hot), token_hot, precision=lax.Precision.HIGHEST)
    weighted_hot = token_hot * gate_weights[0].astype(jnp.float32).reshape(-1)[:, None]
    combine = jnp.dot(jnp.transpose(weighted_hot), slot_hot, precision=lax.Precision.HIGHEST)
    grouped = jnp.dot(
        placing.astype(jnp.bfloat16), normed, preferred_element_type=jnp.float32
    ).astype(jnp.bfloat16)
    width = grouped.shape[1]
    spread = grouped.reshape(expert_count, capacity, rep_count, chunk)
    spread = jnp.transpose(spread, (2, 0, 1, 3)).reshape(rep_count * expert_count, capacity, chunk)
    columns = lax.all_to_all(spread, ("rep",) + EP, 0, 0, tiled=True).reshape(-1, chunk)
    gate_part = jnp.einsum("nd,rdk->rnk", columns, gate_rows, preferred_element_type=jnp.float32)
    up_part = jnp.einsum("nd,rdk->rnk", columns, up_rows, preferred_element_type=jnp.float32)
    parts = jnp.concatenate([gate_part, up_part], axis=2).astype(jnp.bfloat16)
    parts = lax.all_to_all(parts, "rep", 0, 0, tiled=True)
    sums = jnp.sum(parts.astype(jnp.float32), axis=0)
    gate_sum, up_sum = (sums[:, :hidden_width], sums[:, hidden_width:])
    units = (jax.nn.silu(gate_sum) * up_sum).astype(jnp.bfloat16)
    hidden_width = units.shape[1]
    unit_copies = jnp.broadcast_to(units[None], (rep_count,) + units.shape)
    units_all = lax.all_to_all(unit_copies, "rep", 0, 0, tiled=True)
    pieces = jnp.einsum("rnk,rkc->rnc", units_all, down_cols, preferred_element_type=jnp.float32)
    out_cols = jnp.sum(pieces.astype(jnp.bfloat16).astype(jnp.float32), axis=0)
    out_cols = out_cols.astype(jnp.bfloat16)
    out_cols = out_cols.reshape(rep_count * expert_count, capacity, chunk)
    back = lax.all_to_all(out_cols, ("rep",) + EP, 0, 0, tiled=True)
    back = back.reshape(rep_count, expert_count, capacity, chunk)
    served = jnp.transpose(back, (1, 2, 0, 3))
    mixture = jnp.dot(
        combine,
        served.reshape(slot_count, width).astype(jnp.float32),
        precision=lax.Precision.HIGHEST,
    )
    return (residual + mixture)[None]


def solution(mesh):
    rep_n, ep_n = mesh.devices.shape
    fine = Mesh(mesh.devices.reshape(rep_n, ep_n // 2, 2), ("rep", "epo", "core"))
    return jax.shard_map(
        local,
        mesh=fine,
        in_specs=(
            P("rep", None, EP),
            P("rep", EP),
            P("rep", EP, None),
            P(),
            P(),
            P("rep"),
            P("rep", EP, None),
            P(EP, None, None),
            P(EP, None),
            P(),
            P("rep", EP, None),
            P("rep", EP, None),
            P(EP, None, "rep"),
            P(EP, None, "rep"),
            P(EP, "rep", None),
        ),
        out_specs=P("rep", EP, None),
        check_vma=False,
    )
```

profile of v0, /device:TPU:1, one launch (start us, length us, event | category | flops | bytes accessed | tf_op | source)
XLA Modules:
  0.0 342.8 jit_solution(10226278535675166483)
XLA Ops:
  9.8 1.2 reshape.261
  11.0 7.5 %all-to-all-start = ((bf16[8,2,18432]{2,1,0:T(2,128)(2,1)}), bf16[8,2,18432]{2,1,0:T(2,128)(2,1)S(1)}, u32[]{:S(2)}, u32[]{:S(2)}) async-start(bf16[8,2,18432]{2,1,0:T(2,128)(2,1)} %reshape.261), calls=%async_computation | async-start | bytes 1179648 | tf_op jit(solution)/shard_map/all_to_all | solution.py:67
  19.8 11.1 %all-to-all-done = bf16[8,2,18432]{2,1,0:T(2,128)(2,1)S(1)} async-done(((bf16[8,2,18432]{2,1,0:T(2,128)(2,1)}), bf16[8,2,18432]{2,1,0:T(2,128)(2,1)S(1)}, u32[]{:S(2)}, u32[]{:S(2)}) %all-to-all-start) | async-done | bytes 589856 | tf_op jit(solution)/shard_map/all_to_all | solution.py:67
  33.2 1.8 copy.140
  35.1 1.6 copy.150
  36.7 4.4 %all-to-all-start.1 = ((bf16[8,128,896]{2,1,0:T(8,128)(2,1)}), bf16[8,128,896]{2,1,0:T(8,128)(2,1)}, u32[]{:S(2)}, u32[]{:S(2)}) async-start(bf16[8,128,896]{2,1,0:T(8,128)(2,1)} %bitcast.95), calls=%async_computation.1 | async-start | bytes 3670016 | tf_op jit(solution)/shard_map/all_to_all | solution.py:98
  41.1 2.7 copy.115
  43.8 23.2 %all-to-all-done.1 = bf16[8,128,896]{2,1,0:T(8,128)(2,1)} async-done(((bf16[8,128,896]{2,1,0:T(8,128)(2,1)}), bf16[8,128,896]{2,1,0:T(8,128)(2,1)}, u32[]{:S(2)}, u32[]{:S(2)}) %all-to-all-start.1) | async-done | bytes 1835040 | tf_op jit(solution)/shard_map/all_to_all | solution.py:98
  67.0 6.8 %all-to-all-start.2 = ((bf16[8,896,128]{1,2,0:T(8,128)(2,1)}), bf16[8,896,128]{1,2,0:T(8,128)(2,1)}, u32[]{:S(2)}, u32[]{:S(2)}) async-start(bf16[8,896,128]{1,2,0:T(8,128)(2,1)} %copy.115), calls=%async_computation.2 | async-start | bytes 3670016 | tf_op jit(solution)/shard_map/all_to_all | solution.py:99
  73.8 2.7 copy.116
  76.5 25.9 %all-to-all-done.2 = bf16[8,896,128]{1,2,0:T(8,128)(2,1)} async-done(((bf16[8,896,128]{1,2,0:T(8,128)(2,1)}), bf16[8,896,128]{1,2,0:T(8,128)(2,1)}, u32[]{:S(2)}, u32[]{:S(2)}) %all-to-all-start.2) | async-done | bytes 1835040 | tf_op jit(solution)/shard_map/all_to_all | solution.py:99
  102.3 4.4 %all-to-all-start.3 = ((bf16[8,896,128]{1,2,0:T(8,128)(2,1)}), bf16[8,896,128]{1,2,0:T(8,128)(2,1)S(1)}, u32[]{:S(2)}, u32[]{:S(2)}) async-start(bf16[8,896,128]{1,2,0:T(8,128)(2,1)} %copy.116), calls=%async_computation.3 | async-start | bytes 3670016 | tf_op jit(solution)/shard_map/all_to_all | solution.py:102
  108.0 3.9 %fusion.11 = pred[128,4608]{0,1:T(8,128)(4,1)S(1)} fusion(s32[4608]{0:T(1024)S(1)} %sub.25, pred[4608]{0:T(1024)(128)(4,1)S(1)} %and.68, pred[4608]{0:T(1024)(128)(4,1)S(1)} %and.66), kind=kLoop, calls=%fused_computation.21 | loop fusion | flops 1769472 | bytes 617472 | tf_op jit(solution)/shard_map/or | solution.py:115
  111.9 22.9 %all-to-all-done.3 = bf16[8,896,128]{1,2,0:T(8,128)(2,1)S(1)} async-done(((bf16[8,896,128]{1,2,0:T(8,128)(2,1)}), bf16[8,896,128]{1,2,0:T(8,128)(2,1)S(1)}, u32[]{:S(2)}, u32[]{:S(2)}) %all-to-all-start.3) | async-done | bytes 1835040 | tf_op jit(solution)/shard_map/all_to_all | solution.py:102
  134.8 9.8 %all-gather.3.cloned.1.call-done = bf16[4608,576]{1,0:T(8,128)(2,1)} async-done(((bf16[144,576]{1,0:T(8,128)(2,1)}), bf16[4608,576]{1,0:T(8,128)(2,1)}) %all-gather.3.cloned.1.call-update) | async-done | bytes 5308432 | tf_op jit(solution)/shard_map/all_gather | solution.py:93
  144.6 4.7 %fusion.57 = (f32[2,128]{1,0:T(2,128)S(1)}, f32[2,128,4608]{1,2,0:T(8,128)S(1)}) fusion(bf16[4608,576,1]{1,0,2:T(8,128)(2,1)} %bitcast.112, bf16[128,2,576]{0,2,1:T(8,128)(2,1)S(1)} %bitcast.107, pred[128,4608]{0,1:T(8,128)(4,1)S(1)} %fusion.11), kind=kOutput, calls=%fused_computation.92 | convolution fusion | flops 1362493184 | bytes 10912768 | tf_op jit(solution)/shard_map/thc,kc->htk/dot_general | solution.py:118
  150.0 1.5 copy-done.1
  151.5 5.5 %fusion.17 = bf16[128,2,128]{2,0,1:T(8,128)(2,1)S(1)} fusion(bf16[2,512,128]{2,1,0:T(8,128)(2,1)S(1)} %copy-done.11, f32[2,128,4608]{1,2,0:T(8,128)} %copy-done.1, f32[2,128]{1,0:T(2,128)S(1)} %get-tuple-element.13, bf16[4608,576]{1,0:T(8,128)(2,1)} %all-gather.3.cloned.1.call-done, f32[128,2]{0,1:T(2,128)S(1)} %bitcast.111), kind=kOutput, calls=%fused_computation.31 | convolution fusion | flops 1244168192 | bytes 9766912 | tf_op jit(solution)/shard_map/thc,hcv->thv/dot_general | solution.py:129
  157.2 2.7 convolution_convert_fusion.2
  159.9 5.2 %all_to_all.50 = bf16[2,64,7168]{2,1,0:T(8,128)(2,1)S(1)} all-to-all(bf16[2,64,7168]{2,1,0:T(8,128)(2,1)S(1)} %convolution_convert_fusion.2), channel_id=1, replica_groups=mesh['rep'=8,'epo'=16,'core'=2] {'core'}, dimensions={0} | all-to-all | bytes 3670016 | tf_op jit(solution)/shard_map/all_to_all | solution.py:136
  165.9 1.5 convert_element_type.105
  167.4 6.4 %all-to-all-start.5 = ((bf16[16,16,1792]{2,1,0:T(8,128)(2,1)}), bf16[16,16,1792]{2,1,0:T(8,128)(2,1)S(1)}, u32[]{:S(2)}, u32[]{:S(2)}) async-start(bf16[16,16,1792]{2,1,0:T(8,128)(2,1)} %convert_element_type.105), calls=%async_computation.5 | async-start | bytes 1835008 | tf_op jit(solution)/shard_map/all_to_all | solution.py:140
  174.6 22.5 %all-to-all-done.5 = bf16[16,16,1792]{2,1,0:T(8,128)(2,1)S(1)} async-done(((bf16[16,16,1792]{2,1,0:T(8,128)(2,1)}), bf16[16,16,1792]{2,1,0:T(8,128)(2,1)S(1)}, u32[]{:S(2)}, u32[]{:S(2)}) %all-to-all-start.5) | async-done | bytes 917536 | tf_op jit(solution)/shard_map/all_to_all | solution.py:140
  199.5 39.4 %all_to_all.51 = bf16[256,2,896]{2,1,0:T(2,128)(2,1)S(1)} all-to-all(bf16[256,2,896]{2,1,0:T(2,128)(2,1)S(1)} %copy.126), channel_id=1, replica_groups=mesh['rep'=8,'epo'=16,'core'=2] {'rep','epo','core'}, dimensions={0} | all-to-all | bytes 1835008 | tf_op jit(solution)/shard_map/all_to_all | solution.py:174
  239.2 2.9 fusion.12
  242.1 1.3 fusion.13
  243.6 31.2 %all_to_all.52 = bf16[8,512,256]{1,2,0:T(8,128)(2,1)S(1)} all-to-all(bf16[8,512,256]{1,2,0:T(8,128)(2,1)S(1)} %pad_maximum_fusion), channel_id=1, replica_groups=mesh['rep'=8,'epo'=16,'core'=2] {'rep'}, dimensions={0} | all-to-all | bytes 4194304 | tf_op jit(solution)/shard_map/all_to_all | solution.py:178
  275.5 17.4 %all_to_all.53 = bf16[8,512,128]{2,1,0:T(8,128)(2,1)S(1)} all-to-all(bf16[8,512,128]{2,1,0:T(8,128)(2,1)S(1)} %broadcast_in_dim.20), channel_id=1, replica_groups=mesh['rep'=8,'epo'=16,'core'=2] {'rep'}, dimensions={0} | all-to-all | bytes 2097152 | tf_op jit(solution)/shard_map/all_to_all | solution.py:184
  292.8 3.6 %convert_reduce_fusion = bf16[512,896]{1,0:T(8,128)(2,1)S(1)} fusion(bf16[8,512,128]{2,1,0:T(8,128)(2,1)S(1)} %all_to_all.53, bf16[8,128,896]{2,1,0:T(8,128)(2,1)} %all-to-all-done.1), kind=kOutput, calls=%fused_computation.7 | convolution fusion | flops 946405376 | bytes 3801088 | tf_op jit(solution)/shard_map/rnk,rkc->rnc/dot_general | solution.py:185
  296.5 1.3 reshape.245
  297.8 8.3 %all-to-all-start.9 = ((bf16[256,2,896]{2,1,0:T(2,128)(2,1)}), bf16[256,2,896]{2,1,0:T(2,128)(2,1)S(1)}, u32[]{:S(2)}, u32[]{:S(2)}) async-start(bf16[256,2,896]{2,1,0:T(2,128)(2,1)} %reshape.245), calls=%async_computation.9 | async-start | bytes 1835008 | tf_op jit(solution)/shard_map/all_to_all | solution.py:189
  306.4 27.8 %all-to-all-done.9 = bf16[256,2,896]{2,1,0:T(2,128)(2,1)S(1)} async-done(((bf16[256,2,896]{2,1,0:T(2,128)(2,1)}), bf16[256,2,896]{2,1,0:T(2,128)(2,1)S(1)}, u32[]{:S(2)}, u32[]{:S(2)}) %all-to-all-start.9) | async-done | bytes 917536 | tf_op jit(solution)/shard_map/all_to_all | solution.py:189
  (90 shorter events, 15.1 us)
Async XLA Ops:
  6.5 1.3 copy-start
  7.9 11.6 %copy-start.9 = (bf16[1,2304]{1,0:T(2,128)(2,1)S(1)}, bf16[1,2304]{1,0:T(2,128)(2,1)}, u32[]{:S(2)}) copy-start(bf16[1,2304]{1,0:T(2,128)(2,1)} %param.16) | copy-start | bytes 13828
  11.0 19.9 %all-to-all-start = ((bf16[8,2,18432]{2,1,0:T(2,128)(2,1)}), bf16[8,2,18432]{2,1,0:T(2,128)(2,1)S(1)}, u32[]{:S(2)}, u32[]{:S(2)}) async-start(bf16[8,2,18432]{2,1,0:T(2,128)(2,1)} %reshape.261), calls=%async_computation | async-start | bytes 1179648 | tf_op jit(solution)/shard_map/all_to_all | solution.py:67
  18.5 126.0 %all-gather.3.cloned.1.call-start = ((), (), s32[]{:S(2)}) async-start(), calls=%async_computation.10 | async-start | bytes 6082560 | tf_op jit(solution)/shard_map/all_gather | solution.py:93
  36.7 4.5 %copy-start.2 = (bf16[1,7168,128]{2,1,0:T(8,128)(2,1)S(1)}, bf16[1,7168,128]{2,1,0:T(8,128)(2,1)}, u32[]{:S(2)}) copy-start(bf16[1,7168,128]{2,1,0:T(8,128)(2,1)} %param.27) | copy-start | bytes 5505028
  36.7 30.3 %all-to-all-start.1 = ((bf16[8,128,896]{2,1,0:T(8,128)(2,1)}), bf16[8,128,896]{2,1,0:T(8,128)(2,1)}, u32[]{:S(2)}, u32[]{:S(2)}) async-start(bf16[8,128,896]{2,1,0:T(8,128)(2,1)} %bitcast.95), calls=%async_computation.1 | async-start | bytes 3670016 | tf_op jit(solution)/shard_map/all_to_all | solution.py:98
  43.8 30.0 %copy-start.3 = (bf16[1,7168,128]{2,1,0:T(8,128)(2,1)S(1)}, bf16[1,7168,128]{2,1,0:T(8,128)(2,1)}, u32[]{:S(2)}) copy-start(bf16[1,7168,128]{2,1,0:T(8,128)(2,1)} %param.28) | copy-start | bytes 5505028
  67.0 35.4 %all-to-all-start.2 = ((bf16[8,896,128]{1,2,0:T(8,128)(2,1)}), bf16[8,896,128]{1,2,0:T(8,128)(2,1)}, u32[]{:S(2)}, u32[]{:S(2)}) async-start(bf16[8,896,128]{1,2,0:T(8,128)(2,1)} %copy.115), calls=%async_computation.2 | async-start | bytes 3670016 | tf_op jit(solution)/shard_map/all_to_all | solution.py:99
  76.5 31.3 %copy-start.7 = (bf16[1,128,1152]{2,1,0:T(8,128)(2,1)S(1)}, bf16[1,128,1152]{2,1,0:T(8,128)(2,1)}, u32[]{:S(2)}) copy-start(bf16[1,128,1152]{2,1,0:T(8,128)(2,1)} %param.15) | copy-start | bytes 884740
  102.3 32.4 %all-to-all-start.3 = ((bf16[8,896,128]{1,2,0:T(8,128)(2,1)}), bf16[8,896,128]{1,2,0:T(8,128)(2,1)S(1)}, u32[]{:S(2)}, u32[]{:S(2)}) async-start(bf16[8,896,128]{1,2,0:T(8,128)(2,1)} %copy.116), calls=%async_computation.3 | async-start | bytes 3670016 | tf_op jit(solution)/shard_map/all_to_all | solution.py:102
  134.8 14.5 %copy-start.4 = (bf16[8,896,128]{1,2,0:T(8,128)(2,1)}, bf16[8,896,128]{1,2,0:T(8,128)(2,1)S(1)}, u32[]{:S(2)}) copy-start(bf16[8,896,128]{1,2,0:T(8,128)(2,1)S(1)} %all-to-all-done.3) | copy-start | bytes 5505028
  149.3 2.2 copy-start.1
  149.3 2.2 copy-start.11
  165.9 8.0 %copy-start.6 = (bf16[1,4,7168]{2,1,0:T(4,128)(2,1)S(1)}, bf16[1,4,7168]{2,1,0:T(4,128)(2,1)}, u32[]{:S(2)}) copy-start(bf16[1,4,7168]{2,1,0:T(4,128)(2,1)} %param.21) | copy-start | bytes 172036
  165.9 8.1 %copy-start.10 = (s32[1,4,8]{2,1,0:T(4,128)S(1)}, s32[1,4,8]{2,1,0:T(4,128)}, u32[]{:S(2)}) copy-start(s32[1,4,8]{2,1,0:T(4,128)} %param.25) | copy-start | bytes 388
  165.9 8.3 %copy-start.8 = (bf16[7168]{0:T(1024)(128)(2,1)S(1)}, bf16[7168]{0:T(1024)(128)(2,1)}, u32[]{:S(2)}) copy-start(bf16[7168]{0:T(1024)(128)(2,1)} %param.24) | copy-start | bytes 43012
  167.4 29.7 %all-to-all-start.5 = ((bf16[16,16,1792]{2,1,0:T(8,128)(2,1)}), bf16[16,16,1792]{2,1,0:T(8,128)(2,1)S(1)}, u32[]{:S(2)}, u32[]{:S(2)}) async-start(bf16[16,16,1792]{2,1,0:T(8,128)(2,1)} %convert_element_type.105), calls=%async_computation.5 | async-start | bytes 1835008 | tf_op jit(solution)/shard_map/all_to_all | solution.py:140
  239.2 2.9 copy-start.5
  296.5 9.6 %copy-start.12 = (bf16[1,4,8]{2,1,0:T(4,128)(2,1)S(1)}, bf16[1,4,8]{2,1,0:T(4,128)(2,1)}, u32[]{:S(2)}) copy-start(bf16[1,4,8]{2,1,0:T(4,128)(2,1)} %param.26) | copy-start | bytes 196
  297.8 36.5 %all-to-all-start.9 = ((bf16[256,2,896]{2,1,0:T(2,128)(2,1)}), bf16[256,2,896]{2,1,0:T(2,128)(2,1)S(1)}, u32[]{:S(2)}, u32[]{:S(2)}) async-start(bf16[256,2,896]{2,1,0:T(2,128)(2,1)} %reshape.245), calls=%async_computation.9 | async-start | bytes 1835008 | tf_op jit(solution)/shard_map/all_to_all | solution.py:189
Sparse Core Ops, SparseCore 0:
  33.4 111.1 all-gather.2
where the time goes:
time: 344 us; the launch traced here: 343 us
  waiting for transfers between devices  143 us (42%)
  blocking collectives  93.1 us (27%)
  starting transfers between devices  38 us (11%)
  matrix products  24.1 us (7%)
  local copies, waits for them, and re-layouts  21.1 us (6%)
  between operations  14.5 us (4%)
  other arithmetic  8.76 us (3%)
    all_to_all x1, blocking collectives, local(): lax.all_to_all(spread, ('rep',) + EP, 0, 0, tiled=True).reshape(-1, chunk)  39.4 us
    all_to_all x1, blocking collectives, local(): parts = lax.all_to_all(parts, 'rep', 0, 0, tiled=True)  31.2 us
    all_to_all x1, waiting for transfers between devices, local(): back = lax.all_to_all(out_cols, ('rep',) + EP, 0, 0, tiled=True)  27.8 us
    all_to_all x1, waiting for transfers between devices, local(): lax.all_to_all(w_gate[0].reshape(rep_count, chunk, hidden_width), 'rep',...  25.9 us
    all_to_all x1, waiting for transfers between devices, local(): down_cols = lax.all_to_all(down_cols, 'rep', 0, 0, tiled=True)  23.2 us
    all_to_all x1, waiting for transfers between devices, local(): lax.all_to_all(w_up[0].reshape(rep_count, chunk, hidden_width), 'rep', 0,...  22.9 us
    all_to_all x1, waiting for transfers between devices, local(): lax.all_to_all(partial, 'epo', 0, 0, tiled=True).astype(jnp.float32)  22.5 us
    all_to_all x1, blocking collectives, local(): units_all = lax.all_to_all(unit_copies, 'rep', 0, 0, tiled=True)  17.4 us
  transfers between devices with their start and end apart: 7, of which 7 were waited for; matrix products, arithmetic and copies ran while one was open for 5% of the time, Pallas kernels for 0%

commit v1 on v0

--- a/solution.py
+++ b/solution.py
@@ -90,7 +90,11 @@
         axis=0,
     )
     row_count = packed.shape[0]
-    chip_keys = lax.all_gather(packed[None], EP, axis=0, tiled=True)
+    own = packed[None]
+    size = lax.axis_size(EP)
+    blocks = jnp.stack([own for _ in range(size)])
+    blocks = lax.all_to_all(blocks, EP, split_axis=0, concat_axis=0)
+    chip_keys = jnp.concatenate(blocks, axis=0)
     hidden_width, width = (w_down.shape[1], w_down.shape[2])
     chunk = width // rep_count
     down_cols = w_down[0].reshape(hidden_width, rep_count, chunk)

time: 344 us -> 450 us (1.31)
  waiting for transfers between devices: 143 us -> 258 us
  between operations: 14.5 us -> 1.13 us
    all_to_all x0 -> x1, waiting for transfers between devices: none -> 128 us  [local(): blocks = lax.all_to_all(blocks, EP, split_axis=0, concat_axis=0)]
    all_gather x1 -> x0, waiting for transfers between devices: 9.79 us -> none  [local(): chip_keys = lax.all_gather(packed[None], EP, axis=0, tiled=True)]
    all_to_all x0 -> x1, starting transfers between devices: none -> 9.73 us  [local(): blocks = lax.all_to_all(blocks, EP, split_axis=0, concat_axis=0)]
  transfers between devices with their start and end apart: 7 -> 7, of which waited for: 7 -> 7; matrix products, arithmetic and copies ran while one was open for 5% -> 3% of each run, Pallas kernels for 0% -> 0%
where the time goes in v1:
time: 450 us; the launch traced here: 449 us
  waiting for transfers between devices  258 us (57%)
  blocking collectives  91.8 us (20%)
  starting transfers between devices  42.1 us (9%)
  matrix products  25.5 us (6%)
  local copies, waits for them, and re-layouts  22.6 us (5%)
  other arithmetic  8.09 us (2%)
    all_to_all x1, waiting for transfers between devices, local(): blocks = lax.all_to_all(blocks, EP, split_axis=0, concat_axis=0)  128 us
    all_to_all x1, blocking collectives, local(): lax.all_to_all(spread, ('rep',) + EP, 0, 0, tiled=True).reshape(-1, chunk)  37.8 us
    all_to_all x1, blocking collectives, local(): parts = lax.all_to_all(parts, 'rep', 0, 0, tiled=True)  31.3 us
    all_to_all x1, waiting for transfers between devices, local(): back = lax.all_to_all(out_cols, ('rep',) + EP, 0, 0, tiled=True)  27.8 us
    all_to_all x1, waiting for transfers between devices, local(): lax.all_to_all(w_gate[0].reshape(rep_count, chunk, hidden_width), 'rep',...  23.1 us
    all_to_all x1, waiting for transfers between devices, local(): down_cols = lax.all_to_all(down_cols, 'rep', 0, 0, tiled=True)  23.1 us
    all_to_all x1, waiting for transfers between devices, local(): lax.all_to_all(w_up[0].reshape(rep_count, chunk, hidden_width), 'rep', 0,...  22.8 us
    all_to_all x1, waiting for transfers between devices, local(): lax.all_to_all(partial, 'epo', 0, 0, tiled=True).astype(jnp.float32)  22.7 us
  transfers between devices with their start and end apart: 7, of which 7 were waited for; matrix products, arithmetic and copies ran while one was open for 3% of the time, Pallas kernels for 0%

profile of v1, /device:TPU:1, one launch (start us, length us, event | category | flops | bytes accessed | tf_op | source)
XLA Modules:
  0.0 449.4 jit_solution(15101662592000451585)
XLA Ops:
  4.5 7.5 %all-to-all-start = ((bf16[8,2,18432]{2,1,0:T(2,128)(2,1)}), bf16[8,2,18432]{2,1,0:T(2,128)(2,1)S(1)}, u32[]{:S(2)}, u32[]{:S(2)}) async-start(bf16[8,2,18432]{2,1,0:T(2,128)(2,1)} %reshape.266), calls=%async_computation | async-start | bytes 1179648 | tf_op jit(solution)/shard_map/all_to_all | solution.py:67
  12.3 1.5 copy.150
  13.9 10.5 %all-to-all-done = bf16[8,2,18432]{2,1,0:T(2,128)(2,1)S(1)} async-done(((bf16[8,2,18432]{2,1,0:T(2,128)(2,1)}), bf16[8,2,18432]{2,1,0:T(2,128)(2,1)S(1)}, u32[]{:S(2)}, u32[]{:S(2)}) %all-to-all-start) | async-done | bytes 589856 | tf_op jit(solution)/shard_map/all_to_all | solution.py:67
  24.4 4.3 all-to-all-start.2
  28.7 2.7 copy.115
  31.4 23.1 %all-to-all-done.2 = bf16[8,128,896]{2,1,0:T(8,128)(2,1)} async-done(((bf16[8,128,896]{2,1,0:T(8,128)(2,1)}), bf16[8,128,896]{2,1,0:T(8,128)(2,1)}, u32[]{:S(2)}, u32[]{:S(2)}) %all-to-all-start.2) | async-done | bytes 1835040 | tf_op jit(solution)/shard_map/all_to_all | solution.py:102
  54.5 4.3 all-to-all-start.3
  58.8 2.6 copy.116
  61.5 23.1 %all-to-all-done.3 = bf16[8,896,128]{1,2,0:T(8,128)(2,1)} async-done(((bf16[8,896,128]{1,2,0:T(8,128)(2,1)}), bf16[8,896,128]{1,2,0:T(8,128)(2,1)}, u32[]{:S(2)}, u32[]{:S(2)}) %all-to-all-start.3) | async-done | bytes 1835040 | tf_op jit(solution)/shard_map/all_to_all | solution.py:103
  84.6 4.3 all-to-all-start.4
  91.8 22.8 %all-to-all-done.4 = bf16[8,896,128]{1,2,0:T(8,128)(2,1)} async-done(((bf16[8,896,128]{1,2,0:T(8,128)(2,1)}), bf16[8,896,128]{1,2,0:T(8,128)(2,1)}, u32[]{:S(2)}, u32[]{:S(2)}) %all-to-all-start.4) | async-done | bytes 1835040 | tf_op jit(solution)/shard_map/all_to_all | solution.py:106
  114.7 3.0 stack.3
  117.7 9.7 %all-to-all-start.1 = ((bf16[32,1,144,576]{3,2,1,0:T(8,128)(2,1)}), bf16[32,1,144,576]{3,2,1,0:T(8,128)(2,1)}, u32[]{:S(2)}, u32[]{:S(2)}) async-start(bf16[32,1,144,576]{3,2,1,0:T(8,128)(2,1)} %stack.3), calls=%async_computation.1 | async-start | bytes 11796480 | tf_op jit(solution)/shard_map/all_to_all | solution.py:96
  128.7 3.9 fusion.11
  132.6 128.2 %all-to-all-done.1 = bf16[32,1,144,576]{3,2,1,0:T(8,128)(2,1)} async-done(((bf16[32,1,144,576]{3,2,1,0:T(8,128)(2,1)}), bf16[32,1,144,576]{3,2,1,0:T(8,128)(2,1)}, u32[]{:S(2)}, u32[]{:S(2)}) %all-to-all-start.1) | async-done | bytes 5308448 | tf_op jit(solution)/shard_map/all_to_all | solution.py:96
  260.7 4.7 %fusion.57 = (f32[2,128]{1,0:T(2,128)S(1)}, f32[2,128,4608]{1,2,0:T(8,128)S(1)}) fusion(bf16[4608,576,1]{1,0,2:T(8,128)(2,1)} %bitcast.13, bf16[128,2,576]{0,2,1:T(8,128)(2,1)S(1)} %bitcast.107, pred[128,4608]{0,1:T(8,128)(4,1)S(1)} %fusion.11), kind=kOutput, calls=%fused_computation.92 | convolution fusion | flops 1362493184 | bytes 10912768 | tf_op jit(solution)/shard_map/thc,kc->htk/dot_general | solution.py:122
  266.1 1.5 copy-done.2
  267.6 5.5 %fusion.17 = bf16[128,2,128]{2,0,1:T(8,128)(2,1)S(1)} fusion(bf16[2,512,128]{2,1,0:T(8,128)(2,1)S(1)} %copy-done.11, f32[2,128,4608]{1,2,0:T(8,128)} %copy-done.2, f32[2,128]{1,0:T(2,128)S(1)} %get-tuple-element.13, bf16[4608,576]{1,0:T(8,128)(2,1)} %bitcast.10, f32[128,2]{0,1:T(2,128)S(1)} %bitcast.111), kind=kOutput, calls=%fused_computation.31 | convolution fusion | flops 1244168192 | bytes 9766912 | tf_op jit(solution)/shard_map/thc,hcv->thv/dot_general | solution.py:133
  273.3 2.7 convolution_convert_fusion.2
  276.0 5.3 %all_to_all.55 = bf16[2,64,7168]{2,1,0:T(8,128)(2,1)S(1)} all-to-all(bf16[2,64,7168]{2,1,0:T(8,128)(2,1)S(1)} %convolution_convert_fusion.2), channel_id=1, replica_groups=mesh['rep'=8,'epo'=16,'core'=2] {'core'}, dimensions={0} | all-to-all | bytes 3670016 | tf_op jit(solution)/shard_map/all_to_all | solution.py:140
  282.2 1.5 convert_element_type.105
  283.8 3.6 all-to-all-start.6
  288.1 22.7 %all-to-all-done.6 = bf16[16,16,1792]{2,1,0:T(8,128)(2,1)S(1)} async-done(((bf16[16,16,1792]{2,1,0:T(8,128)(2,1)}), bf16[16,16,1792]{2,1,0:T(8,128)(2,1)S(1)}, u32[]{:S(2)}, u32[]{:S(2)}) %all-to-all-start.6) | async-done | bytes 917536 | tf_op jit(solution)/shard_map/all_to_all | solution.py:144
  313.2 37.8 %all_to_all.56 = bf16[256,2,896]{2,1,0:T(2,128)(2,1)S(1)} all-to-all(bf16[256,2,896]{2,1,0:T(2,128)(2,1)S(1)} %copy.126), channel_id=1, replica_groups=mesh['rep'=8,'epo'=16,'core'=2] {'rep','epo','core'}, dimensions={0} | all-to-all | bytes 1835008 | tf_op jit(solution)/shard_map/all_to_all | solution.py:178
  351.3 2.8 fusion.12
  354.1 2.8 fusion.13
  357.1 31.3 %all_to_all.57 = bf16[8,512,256]{1,2,0:T(8,128)(2,1)S(1)} all-to-all(bf16[8,512,256]{1,2,0:T(8,128)(2,1)S(1)} %pad_maximum_fusion), channel_id=1, replica_groups=mesh['rep'=8,'epo'=16,'core'=2] {'rep'}, dimensions={0} | all-to-all | bytes 4194304 | tf_op jit(solution)/shard_map/all_to_all | solution.py:182
  389.0 17.4 %all_to_all.58 = bf16[8,512,128]{2,1,0:T(8,128)(2,1)S(1)} all-to-all(bf16[8,512,128]{2,1,0:T(8,128)(2,1)S(1)} %broadcast_in_dim.17), channel_id=1, replica_groups=mesh['rep'=8,'epo'=16,'core'=2] {'rep'}, dimensions={0} | all-to-all | bytes 2097152 | tf_op jit(solution)/shard_map/all_to_all | solution.py:188
  406.3 3.6 convert_reduce_fusion
  410.0 1.3 reshape.251
  411.2 8.3 %all-to-all-start.10 = ((bf16[256,2,896]{2,1,0:T(2,128)(2,1)}), bf16[256,2,896]{2,1,0:T(2,128)(2,1)S(1)}, u32[]{:S(2)}, u32[]{:S(2)}) async-start(bf16[256,2,896]{2,1,0:T(2,128)(2,1)} %reshape.251), calls=%async_computation.10 | async-start | bytes 1835008 | tf_op jit(solution)/shard_map/all_to_all | solution.py:193
  419.9 27.8 %all-to-all-done.10 = bf16[256,2,896]{2,1,0:T(2,128)(2,1)S(1)} async-done(((bf16[256,2,896]{2,1,0:T(2,128)(2,1)}), bf16[256,2,896]{2,1,0:T(2,128)(2,1)S(1)}, u32[]{:S(2)}, u32[]{:S(2)}) %all-to-all-start.10) | async-done | bytes 917536 | tf_op jit(solution)/shard_map/all_to_all | solution.py:193
  (90 shorter events, 16.0 us)
Async XLA Ops:
  0.0 1.3 copy-start
  1.4 10.6 %copy-start.3 = (bf16[1,128,7168]{2,1,0:T(8,128)(2,1)S(1)}, bf16[1,128,7168]{2,1,0:T(8,128)(2,1)}, u32[]{:S(2)}) copy-start(bf16[1,128,7168]{2,1,0:T(8,128)(2,1)} %param.29) | copy-start | bytes 5505028
  4.5 19.9 %all-to-all-start = ((bf16[8,2,18432]{2,1,0:T(2,128)(2,1)}), bf16[8,2,18432]{2,1,0:T(2,128)(2,1)S(1)}, u32[]{:S(2)}, u32[]{:S(2)}) async-start(bf16[8,2,18432]{2,1,0:T(2,128)(2,1)} %reshape.266), calls=%async_computation | async-start | bytes 1179648 | tf_op jit(solution)/shard_map/all_to_all | solution.py:67
  13.8 14.9 %copy-start.4 = (bf16[1,7168,128]{2,1,0:T(8,128)(2,1)S(1)}, bf16[1,7168,128]{2,1,0:T(8,128)(2,1)}, u32[]{:S(2)}) copy-start(bf16[1,7168,128]{2,1,0:T(8,128)(2,1)} %param.27) | copy-start | bytes 5505028
  24.4 30.1 %all-to-all-start.2 = ((bf16[8,128,896]{2,1,0:T(8,128)(2,1)}), bf16[8,128,896]{2,1,0:T(8,128)(2,1)}, u32[]{:S(2)}, u32[]{:S(2)}) async-start(bf16[8,128,896]{2,1,0:T(8,128)(2,1)} %bitcast.95), calls=%async_computation.2 | async-start | bytes 3670016 | tf_op jit(solution)/shard_map/all_to_all | solution.py:102
  31.4 27.4 %copy-start.5 = (bf16[1,7168,128]{2,1,0:T(8,128)(2,1)S(1)}, bf16[1,7168,128]{2,1,0:T(8,128)(2,1)}, u32[]{:S(2)}) copy-start(bf16[1,7168,128]{2,1,0:T(8,128)(2,1)} %param.28) | copy-start | bytes 5505028
  54.5 30.1 %all-to-all-start.3 = ((bf16[8,896,128]{1,2,0:T(8,128)(2,1)}), bf16[8,896,128]{1,2,0:T(8,128)(2,1)}, u32[]{:S(2)}, u32[]{:S(2)}) async-start(bf16[8,896,128]{1,2,0:T(8,128)(2,1)} %copy.115), calls=%async_computation.3 | async-start | bytes 3670016 | tf_op jit(solution)/shard_map/all_to_all | solution.py:103
  61.5 28.3 %copy-start.9 = (bf16[1,2304]{1,0:T(2,128)(2,1)S(1)}, bf16[1,2304]{1,0:T(2,128)(2,1)}, u32[]{:S(2)}) copy-start(bf16[1,2304]{1,0:T(2,128)(2,1)} %param.16) | copy-start | bytes 13828
  84.6 30.1 %all-to-all-start.4 = ((bf16[8,896,128]{1,2,0:T(8,128)(2,1)}), bf16[8,896,128]{1,2,0:T(8,128)(2,1)}, u32[]{:S(2)}, u32[]{:S(2)}) async-start(bf16[8,896,128]{1,2,0:T(8,128)(2,1)} %copy.116), calls=%async_computation.4 | async-start | bytes 3670016 | tf_op jit(solution)/shard_map/all_to_all | solution.py:106
  117.7 10.7 %copy-start.7 = (bf16[1,128,1152]{2,1,0:T(8,128)(2,1)S(1)}, bf16[1,128,1152]{2,1,0:T(8,128)(2,1)}, u32[]{:S(2)}) copy-start(bf16[1,128,1152]{2,1,0:T(8,128)(2,1)} %param.15) | copy-start | bytes 884740
  117.7 143.0 %all-to-all-start.1 = ((bf16[32,1,144,576]{3,2,1,0:T(8,128)(2,1)}), bf16[32,1,144,576]{3,2,1,0:T(8,128)(2,1)}, u32[]{:S(2)}, u32[]{:S(2)}) async-start(bf16[32,1,144,576]{3,2,1,0:T(8,128)(2,1)} %stack.3), calls=%async_computation.1 | async-start | bytes 11796480 | tf_op jit(solution)/shard_map/all_to_all | solution.py:96
  265.4 2.2 copy-start.2
  265.5 2.2 copy-start.11
  282.2 5.2 %copy-start.6 = (bf16[1,4,7168]{2,1,0:T(4,128)(2,1)S(1)}, bf16[1,4,7168]{2,1,0:T(4,128)(2,1)}, u32[]{:S(2)}) copy-start(bf16[1,4,7168]{2,1,0:T(4,128)(2,1)} %param.21) | copy-start | bytes 172036
  282.2 5.3 %copy-start.10 = (s32[1,4,8]{2,1,0:T(4,128)S(1)}, s32[1,4,8]{2,1,0:T(4,128)}, u32[]{:S(2)}) copy-start(s32[1,4,8]{2,1,0:T(4,128)} %param.25) | copy-start | bytes 388
  282.2 5.5 %copy-start.8 = (bf16[7168]{0:T(1024)(128)(2,1)S(1)}, bf16[7168]{0:T(1024)(128)(2,1)}, u32[]{:S(2)}) copy-start(bf16[7168]{0:T(1024)(128)(2,1)} %param.24) | copy-start | bytes 43012
  283.8 27.1 %all-to-all-start.6 = ((bf16[16,16,1792]{2,1,0:T(8,128)(2,1)}), bf16[16,16,1792]{2,1,0:T(8,128)(2,1)S(1)}, u32[]{:S(2)}, u32[]{:S(2)}) async-start(bf16[16,16,1792]{2,1,0:T(8,128)(2,1)} %convert_element_type.105), calls=%async_computation.6 | async-start | bytes 1835008 | tf_op jit(solution)/shard_map/all_to_all | solution.py:144
  410.0 9.6 %copy-start.12 = (bf16[1,4,8]{2,1,0:T(4,128)(2,1)S(1)}, bf16[1,4,8]{2,1,0:T(4,128)(2,1)}, u32[]{:S(2)}) copy-start(bf16[1,4,8]{2,1,0:T(4,128)(2,1)} %param.26) | copy-start | bytes 196
  411.2 36.5 %all-to-all-start.10 = ((bf16[256,2,896]{2,1,0:T(2,128)(2,1)}), bf16[256,2,896]{2,1,0:T(2,128)(2,1)S(1)}, u32[]{:S(2)}, u32[]{:S(2)}) async-start(bf16[256,2,896]{2,1,0:T(2,128)(2,1)} %reshape.251), calls=%async_computation.10 | async-start | bytes 1835008 | tf_op jit(solution)/shard_map/all_to_all | solution.py:193
  447.8 1.6 copy-start.1
